TPU v7x, 128 devices: a whole 4x4x4 slice. The times are simulated.
128 devices in a mesh: segment: 4 (over x), dp: 32 (over y, z, core).
Axes of the slice: x: 4, y: 4, z: 4, core: 2. Of those that a mesh axis runs over, the one named last changes fastest.
Arguments:
- query_states: bfloat16 [1024, 32, 768], P('dp'), may hold values from -40 to 40
- passage_states: bfloat16 [512, 64, 768], P('dp'), may hold values from -40 to 40
- query_tokens: int32 [1024, 32], P('dp'), may hold values from 0 to 32099, as said below
- passage_tokens: int32 [512, 64], P('dp'), may hold values from 0 to 32099, as said below
- ff_gains: float32 [2, 768], replicated, may hold values from 0.1 to 1.9
- out_gains: float32 [2, 768], replicated, may hold values from 0.1 to 1.9
- w_gate: bfloat16 [2, 768, 2048], P(None, None, 'segment'), may hold values from -0.21875 to 0.21875
- w_up: bfloat16 [2, 768, 2048], P(None, None, 'segment'), may hold values from -0.21875 to 0.21875
- w_down: bfloat16 [2, 2048, 768], P(None, 'segment'), may hold values from -1 to 1
- w_proj: bfloat16 [2, 768, 768], replicated, may hold values from -0.21875 to 0.21875
- positive_ids: int32 [1024], P('dp'), may hold values from 0 to 511
- negative_ids: int32 [1024, 15], P('dp'), may hold values from 0 to 511
- negative_counts: int32 [1024], P('dp'), may hold values from 1 to 15, 7680 in all
Outputs:
- grad_gate: float32 [2, 768, 2048], P(None, 'dp', 'segment')
- grad_up: float32 [2, 768, 2048], P(None, 'dp', 'segment')
- grad_down: float32 [2, 2048, 768], P(None, 'segment', 'dp')
Inputs may be any that keep to these rules, and one draw needn't show every extreme that they name: `query_tokens`: each row holds token ids of 1 or more followed by zeros, at least 8 nonzero ids; the first row has no zeros. `passage_tokens`: each row holds token ids of 1 or more followed by zeros, at least 16 nonzero ids; the first row has no zeros. Only the first negative_counts[i] entries of row i are used; the counts sum to 7680.
All inputs are finite; a program needn't handle non-finite values. No bound on the sum of `negative_counts` on one device may be relied on, other than what follows from the above.
Results may differ from a plain program's by a relative error of at most 0.012.
Values may be sent and summed in bfloat16 or wider, within the bound.
No kernel may reach another device: no remote copies, remote signals or barrier semaphores. Data moves between devices by JAX's collectives and lax.ppermute only.
A program may use at most 128 MiB of HBM per device.

v0:
```python
import jax
import jax.numpy as jnp
from jax import lax
from jax.sharding import PartitionSpec as P

score_temp = 0.05
rank_temp = 1.0
recall_depth = 5.0
loss_scale = 16.0
norm_eps = 1e-06


def inverse_rms(values):
    return lax.rsqrt(jnp.mean(values * values, axis=-1, keepdims=True) + norm_eps)


def normed_input(states, ff_gain):
    widened = states.astype(jnp.float32)
    return (widened * inverse_rms(widened) * ff_gain).astype(jnp.bfloat16)


def pooled_embedding(summed, tokens, out_gain, proj_weight):
    normed = summed * inverse_rms(summed) * out_gain
    token_mask = (tokens != 0).astype(jnp.float32)[:, :, None]
    pooled = jnp.sum(normed * token_mask, axis=1) / jnp.sum(token_mask, axis=1)
    projected = jnp.dot(pooled, proj_weight.astype(jnp.float32), precision=lax.Precision.HIGHEST)
    return projected * lax.rsqrt(jnp.sum(projected * projected, axis=-1, keepdims=True) + norm_eps)


def recall_loss(scores, valid_mask):
    margins = (scores[:, 1:] - scores[:, :1]) / score_temp
    soft_ranks = 1.0 + jnp.sum(jax.nn.sigmoid(margins) * valid_mask, axis=1)
    return loss_scale * jnp.sum(jax.nn.sigmoid((soft_ranks - recall_depth - 0.5) / rank_temp))


def contract(left, right):
    return lax.dot_general(
        left, right, (((0,), (0,)), ((), ())), preferred_element_type=jnp.float32
    )


def natural_order(gathered, segments, groups, per_device):
    model_width = gathered.shape[-1]
    shaped = gathered.reshape(segments, groups, per_device, model_width)
    return jnp.transpose(shaped, (1, 0, 2, 3)).reshape(-1, model_width)


def score_grads_of(scores, counts):
    slots = scores.shape[1] - 1
    valid_mask = (
        lax.broadcasted_iota(jnp.int32, (scores.shape[0], slots), 1) < counts[:, None]
    ).astype(jnp.float32)
    return jax.grad(recall_loss)(scores, valid_mask)


def body(
    query_states,
    passage_states,
    query_tokens,
    passage_tokens,
    ff_gains,
    out_gains,
    w_gate,
    w_up,
    w_down,
    w_proj,
    positive_ids,
    negative_ids,
    negative_counts,
):
    segments = lax.axis_size("segment")
    groups = lax.axis_size("dp")
    segment_index = lax.axis_index("segment")
    model_width = query_states.shape[-1]
    query_dev = query_states.shape[0] // segments
    passage_dev = passage_states.shape[0] // segments

    def forward_part(states, tower_index):
        normed = normed_input(states, ff_gains[tower_index]).reshape(-1, model_width)
        gate_pre = jnp.dot(normed, w_gate[tower_index], preferred_element_type=jnp.float32)
        up_pre = jnp.dot(normed, w_up[tower_index], preferred_element_type=jnp.float32)
        activated, gelu_back = jax.vjp(jax.nn.gelu, gate_pre)
        hidden = (activated * up_pre).astype(jnp.bfloat16)
        branch = jnp.dot(hidden, w_down[tower_index], preferred_element_type=jnp.float32).reshape(
            states.shape
        )
        return (normed, up_pre, activated, gelu_back, hidden, branch)

    def own_rows(values, per_device):
        return lax.dynamic_slice_in_dim(values, segment_index * per_device, per_device, 0)

    def head_of(tokens, tower_index):
        return lambda summed: pooled_embedding(
            summed, tokens, out_gains[tower_index], w_proj[tower_index]
        )

    query_parts = forward_part(query_states, 0)
    passage_parts = forward_part(passage_states, 1)
    query_branch, passage_branch = (
        lax.psum_scatter(query_parts[5], "segment", scatter_dimension=0, tiled=True),
        lax.psum_scatter(passage_parts[5], "segment", scatter_dimension=0, tiled=True),
    )
    query_embed, query_back = jax.vjp(
        head_of(own_rows(query_tokens, query_dev), 0),
        own_rows(query_states, query_dev).astype(jnp.float32) + query_branch,
    )
    passage_embed, passage_back = jax.vjp(
        head_of(own_rows(passage_tokens, passage_dev), 1),
        own_rows(passage_states, passage_dev).astype(jnp.float32) + passage_branch,
    )
    query_round = query_embed.astype(jnp.bfloat16)
    passage_round = passage_embed.astype(jnp.bfloat16)
    id_radix = 256
    own_ids = jnp.concatenate(
        [own_rows(positive_ids, query_dev)[:, None], own_rows(negative_ids, query_dev)], axis=1
    )
    slots = own_ids.shape[1]
    own_meta = jnp.concatenate(
        [own_ids // id_radix, own_ids % id_radix, own_rows(negative_counts, query_dev)[:, None]],
        axis=1,
    ).astype(jnp.bfloat16)
    meta_width = own_meta.shape[1]
    meta_rows = -(-query_dev * meta_width // model_width)
    meta_flat = jnp.pad(
        own_meta.reshape(-1), (0, meta_rows * model_width - query_dev * meta_width)
    ).reshape(meta_rows, model_width)
    packed = jnp.concatenate([query_round, passage_round, meta_flat], axis=0)
    gathered = lax.all_gather(packed, ("dp", "segment"), axis=0, tiled=False)
    gathered = gathered.reshape(groups, segments, -1, model_width)
    query_all = gathered[:, :, :query_dev].reshape(-1, model_width)
    passage_all = gathered[:, :, query_dev : query_dev + passage_dev].reshape(-1, model_width)
    meta_all = (
        gathered[:, :, query_dev + passage_dev :]
        .reshape(groups, segments, -1)[:, :, : query_dev * meta_width]
        .reshape(-1, meta_width)
        .astype(jnp.int32)
    )
    cand_all = meta_all[:, :slots] * id_radix + meta_all[:, slots : 2 * slots]
    counts_all = meta_all[:, 2 * slots]
    passage_total = passage_all.shape[0]
    all_scores = lax.dot_general(
        query_all, passage_all, (((1,), (1,)), ((), ())), preferred_element_type=jnp.float32
    )
    scores = jnp.take_along_axis(all_scores, cand_all, axis=1)
    score_grads = score_grads_of(scores, counts_all)
    dp_index = lax.axis_index("dp")
    query_start = (dp_index * segments + segment_index) * query_dev
    passage_start = (dp_index * segments + segment_index) * passage_dev
    own_cand = lax.dynamic_slice_in_dim(cand_all, query_start, query_dev, 0)
    own_grads = lax.dynamic_slice_in_dim(score_grads, query_start, query_dev, 0)
    every_id = lax.broadcasted_iota(jnp.int32, (1, 1, passage_total), 2)
    query_coef = jnp.sum(
        jnp.where(own_cand[:, :, None] == every_id, own_grads[:, :, None], 0.0), axis=1
    )
    own_passages = passage_start + lax.broadcasted_iota(jnp.int32, (1, 1, passage_dev), 2)
    passage_coef = jnp.sum(
        jnp.where(cand_all[:, :, None] == own_passages, score_grads[:, :, None], 0.0), axis=1
    )
    query_grad = jnp.dot(
        query_coef, passage_all.astype(jnp.float32), precision=lax.Precision.HIGHEST
    )
    passage_grad = lax.dot_general(
        passage_coef,
        query_all.astype(jnp.float32),
        (((0,), (0,)), ((), ())),
        precision=lax.Precision.HIGHEST,
        preferred_element_type=jnp.float32,
    )
    query_share = query_back(query_grad)[0].astype(jnp.bfloat16)
    passage_share = passage_back(passage_grad)[0].astype(jnp.bfloat16)
    query_rows, passage_rows = (
        lax.all_gather(query_share, "segment", axis=0, tiled=True),
        lax.all_gather(passage_share, "segment", axis=0, tiled=True),
    )

    def backward_part(tower_parts, row_grads, tower_index):
        normed, up_pre, activated, gelu_back, hidden, branch = tower_parts
        flat_grad = row_grads.reshape(-1, model_width)
        hidden_grad = lax.dot_general(
            flat_grad,
            w_down[tower_index],
            (((1,), (1,)), ((), ())),
            preferred_element_type=jnp.float32,
        )
        gate_grad = gelu_back(hidden_grad * up_pre)[0].astype(jnp.bfloat16)
        up_grad = (hidden_grad * activated).astype(jnp.bfloat16)
        return (normed, gate_grad, up_grad, hidden, flat_grad)

    towers_back = (
        backward_part(query_parts, query_rows, 0),
        backward_part(passage_parts, passage_rows, 1),
    )

    def weight_terms():
        matrices = [[], [], []]
        for normed, gate_grad, up_grad, hidden, flat_grad in towers_back:
            matrices[0].append(contract(normed, gate_grad))
            matrices[1].append(contract(normed, up_grad))
            matrices[2].append(contract(flat_grad, hidden))
        return jnp.stack([jnp.stack(pieces, axis=1) for pieces in matrices], axis=1)

    summed_grads = lax.psum_scatter(weight_terms(), "dp", scatter_dimension=0, tiled=True)
    grad_gate = jnp.transpose(summed_grads[:, 0], (1, 0, 2))
    grad_up = jnp.transpose(summed_grads[:, 1], (1, 0, 2))
    grad_down = jnp.transpose(summed_grads[:, 2], (1, 2, 0))
    return (grad_gate, grad_up, grad_down)


def solution(mesh):
    return jax.shard_map(
        body,
        mesh=mesh,
        in_specs=(
            P("dp", None, None),
            P("dp", None, None),
            P("dp", None),
            P("dp", None),
            P(),
            P(),
            P(None, None, "segment"),
            P(None, None, "segment"),
            P(None, "segment", None),
            P(),
            P("dp"),
            P("dp", None),
            P("dp"),
        ),
        out_specs=(P(None, "dp", "segment"), P(None, "dp", "segment"), P(None, "segment", "dp")),
        check_vma=False,
    )
```

profile of v0, /device:TPU:0, one launch (start us, length us, event | category | flops | bytes accessed | tf_op | source)
XLA Modules:
  0.0 496.1 jit_solution(10540428919395859232)
XLA Ops:
  7.2 0.8 slice_reduce_fusion.5
  8.1 1.9 fusion
  10.5 1.0 fusion.56
  11.6 0.8 copy-done.56
  12.5 2.6 multiply_convert_fusion.3
  15.1 1.0 copy-done.18
  16.1 2.6 fusion.50
  18.8 1.3 copy-done.4
  20.5 0.4 fusion.5
  20.9 0.6 copy-done.55
  21.5 1.0 fusion.48
  22.5 0.4 copy-done.57
  22.9 2.6 multiply_convert_fusion.2
  25.6 1.0 copy-done.19
  26.5 2.6 fusion.42
  29.3 0.6 copy-done.44
  30.6 0.8 fusion.119
  31.4 0.8 fusion.117
  32.3 27.3 %reduce-scatter.4.cloned.1.call-done = f32[8,32,768]{2,1,0:T(8,128)} async-done(((f32[32,32,768]{2,1,0:T(8,128)}), f32[8,32,768]{2,1,0:T(8,128)}) %reduce-scatter.4.cloned.1.call-update) | async-done | bytes 786448 | tf_op jit(solution)/shard_map/reduce_scatter | solution.py:100
  59.6 1.5 multiply_reduce_fusion.5
  61.1 1.4 multiply_reduce_fusion.4
  62.6 0.7 multiply_reduce_fusion.7
  63.4 36.7 %reduce-scatter.6.cloned.1.call-done = f32[4,64,768]{2,1,0:T(8,128)} async-done(((f32[16,64,768]{2,1,0:T(8,128)}), f32[4,64,768]{2,1,0:T(8,128)}) %reduce-scatter.6.cloned.1.call-update) | async-done | bytes 786448 | tf_op jit(solution)/shard_map/reduce_scatter | solution.py:101
  100.0 1.5 multiply_reduce_fusion.3
  101.6 1.4 multiply_reduce_fusion.2
  103.0 0.7 multiply_reduce_fusion.9
  103.9 0.5 copy-done.60
  104.4 0.6 maximum_bitcast_fusion.3
  105.3 65.5 %all-gather.10.cloned.1.call-done = bf16[128,13,768]{2,1,0:T(8,128)(2,1)} async-done(((bf16[1,13,768]{2,1,0:T(8,128)(2,1)}), bf16[128,13,768]{2,1,0:T(8,128)(2,1)}) %all-gather.10.cloned.1.call-update) | async-done | bytes 2555920 | tf_op jit(solution)/shard_map/all_gather | solution.py:128
  170.8 1.8 slice.100
  173.2 1.0 slice_reduce_fusion.1
  174.1 1.0 bitcast_or_fusion
  175.2 1.6 slice.106
  176.8 1.3 slice.105
  178.5 0.9 copy-done.9
  179.4 2.4 fusion.121
  181.8 129.5 %gather_fusion = f32[16384]{0:T(1024)S(1)} fusion(f32[1024,512]{1,0:T(8,128)S(1)} %fusion.121, s32[16384]{0:T(1024)S(1)} %reshape.165), kind=kCustom, calls=%fused_computation | custom fusion | bytes 262144 | tf_op jit(solution)/shard_map/jit(take_along_axis)/gather | solution.py:144
  312.0 0.6 select_reduce_fusion
  312.6 1.0 fusion.115
  313.6 1.0 copy.42
  314.7 0.8 fusion.85
  315.6 1.7 multiply_reduce_fusion.6
  317.3 2.3 fusion.28
  320.0 1.0 fusion.40
  321.3 1.3 pad_add_fusion
  322.9 2.4 multiply_reduce_fusion.8
  325.4 2.3 fusion.31
  328.1 1.1 fusion.41
  329.5 15.6 %all-gather.6.cloned.1.call-done = bf16[32,32,768]{2,1,0:T(8,128)(2,1)} async-done(((bf16[8,32,768]{2,1,0:T(8,128)(2,1)}), bf16[32,32,768]{2,1,0:T(8,128)(2,1)}) %all-gather.6.cloned.1.call-update) | async-done | bytes 1572880 | tf_op jit(solution)/shard_map/all_gather | solution.py:172
  345.0 2.9 convolution_bitcast_fusion.1
  347.9 2.3 fusion.52
  350.3 22.7 %all-gather.8.cloned.1.call-done = bf16[16,64,768]{2,1,0:T(8,128)(2,1)} async-done(((bf16[4,64,768]{2,1,0:T(8,128)(2,1)}), bf16[16,64,768]{2,1,0:T(8,128)(2,1)}) %all-gather.8.cloned.1.call-update) | async-done | bytes 1572880 | tf_op jit(solution)/shard_map/all_gather | solution.py:173
  373.0 2.8 convolution_bitcast_fusion
  375.9 1.0 fusion.44
  377.3 0.7 copy-done.64
  377.9 1.1 convolution_bitcast_fusion.3
  379.1 0.4 copy-done.69
  379.5 2.4 convolution_bitcast_fusion.5
  381.9 1.1 convolution_bitcast_fusion.2
  383.1 0.4 copy-done.70
  383.5 2.4 convolution_bitcast_fusion.4
  386.8 4.8 pad_maximum_fusion
  391.7 95.9 %reduce-scatter.8.cloned.1.call-done = f32[24,3,2,512]{3,0,2,1:T(8,128)} async-done(((f32[768,3,2,512]{3,0,2,1:T(8,128)}), f32[24,3,2,512]{3,0,2,1:T(8,128)}) %reduce-scatter.8.cloned.1.call-update) | async-done | bytes 294928 | tf_op jit(solution)/shard_map/reduce_scatter | solution.py:202
  487.5 1.7 slice_bitcast_fusion
  (189 shorter events, 6.9 us)
Async XLA Ops:
  7.2 23.0 %copy-start = (s32[32,15]{0,1:T(8,128)S(1)}, s32[32,15]{0,1:T(8,128)}, u32[]{:S(2)}) copy-start(s32[32,15]{0,1:T(8,128)} %param.24) | copy-start | bytes 5764
  7.2 2.8 copy-start.2
  7.2 52.4 %reduce-scatter.4.cloned.1.call-start = ((), (), s32[]{:S(2)}) async-start(), calls=%async_computation.3 | async-start | bytes 3932160 | tf_op jit(solution)/shard_map/reduce_scatter | solution.py:100
  8.1 2.4 copy-start.54
  10.5 2.0 copy-start.56
  12.4 2.6 copy-start.65
  12.5 3.6 copy-start.11
  18.7 81.3 %reduce-scatter.6.cloned.1.call-start = ((), (), s32[]{:S(2)}) async-start(), calls=%async_computation.4 | async-start | bytes 3932160 | tf_op jit(solution)/shard_map/reduce_scatter | solution.py:101
  20.9 1.6 copy-start.16
  22.9 2.6 copy-start.67
  22.9 3.6 copy-start.12
  29.2 3.0 copy-start.41
  29.2 141.6 %all-gather.10.cloned.1.call-start = ((), (), s32[]{:S(2)}) async-start(), calls=%async_computation.8 | async-start | bytes 3170304 | tf_op jit(solution)/shard_map/all_gather | solution.py:128
  31.4 70.2 %copy-start.35 = (f32[4,64]{1,0:T(4,128)}, f32[4,64]{1,0:T(4,128)S(1)}, u32[]{:S(2)}) copy-start(f32[4,64]{1,0:T(4,128)S(1)} %get-tuple-element.14) | copy-start | bytes 3076
  31.4 71.6 %copy-start.46 = (f32[4]{0:T(128)}, f32[4]{0:T(128)S(1)}, u32[]{:S(2)}) copy-start(f32[4]{0:T(128)S(1)} %get-tuple-element.13) | copy-start | bytes 52
  32.2 69.3 %copy-start.26 = (f32[8,32]{1,0:T(8,128)}, f32[8,32]{1,0:T(8,128)S(1)}, u32[]{:S(2)}) copy-start(f32[8,32]{1,0:T(8,128)S(1)} %get-tuple-element.12) | copy-start | bytes 3076
  32.2 69.3 %copy-start.50 = (f32[8]{0:T(128)}, f32[8]{0:T(128)S(1)}, u32[]{:S(2)}) copy-start(f32[8]{0:T(128)S(1)} %get-tuple-element.11) | copy-start | bytes 100
  32.3 69.3 %copy-start.24 = (f32[768]{0:T(1024)}, f32[768]{0:T(1024)S(1)}, u32[]{:S(2)}) copy-start(f32[768]{0:T(1024)S(1)} %get-tuple-element.5) | copy-start | bytes 9220
  32.3 69.3 %copy-start.22 = (f32[768]{0:T(1024)}, f32[768]{0:T(1024)S(1)}, u32[]{:S(2)}) copy-start(f32[768]{0:T(1024)S(1)} %get-tuple-element.6) | copy-start | bytes 9220
  59.6 3.0 copy-start.52
  61.1 1.5 copy-start.33
  61.1 1.4 copy-start.31
  63.3 109.3 %copy-start.20 = (f32[8,768]{1,0:T(8,128)}, f32[8,768]{1,0:T(8,128)S(1)}, u32[]{:S(2)}) copy-start(f32[8,768]{1,0:T(8,128)S(1)} %get-tuple-element.27) | copy-start | bytes 73732
  63.3 109.3 %copy-start.62 = (f32[8]{0:T(128)}, f32[8]{0:T(128)S(1)}, u32[]{:S(2)}) copy-start(f32[8]{0:T(128)S(1)} %get-tuple-element.26) | copy-start | bytes 100
  63.4 109.3 %copy-start.42 = (f32[8]{0:T(128)}, f32[8]{0:T(128)S(1)}, u32[]{:S(2)}) copy-start(f32[8]{0:T(128)S(1)} %add_rsqrt_fusion.3) | copy-start | bytes 100
  100.0 3.0 copy-start.53
  101.5 71.2 %copy-start.39 = (f32[4,64]{1,0:T(4,128)}, f32[4,64]{1,0:T(4,128)S(1)}, u32[]{:S(2)}) copy-start(f32[4,64]{1,0:T(4,128)S(1)} %multiply_reduce_fusion.3) | copy-start | bytes 3076
  101.6 71.2 %copy-start.37 = (f32[4,64]{1,0:T(4,128)}, f32[4,64]{1,0:T(4,128)S(1)}, u32[]{:S(2)}) copy-start(f32[4,64]{1,0:T(4,128)S(1)} %fusion.94) | copy-start | bytes 3076
  103.8 69.0 %copy-start.48 = (f32[4]{0:T(128)}, f32[4]{0:T(128)S(1)}, u32[]{:S(2)}) copy-start(f32[4]{0:T(128)S(1)} %add_rsqrt_fusion.2) | copy-start | bytes 52
  105.1 240.0 %all-gather.6.cloned.1.call-start = ((), (), s32[]{:S(2)}) async-start(), calls=%async_computation.5 | async-start | bytes 1966080 | tf_op jit(solution)/shard_map/all_gather | solution.py:172
  173.2 3.6 copy-start.10
  181.8 129.7 %copy-start.8 = (s32[1024,16]{1,0:T(8,128)S(1)}, s32[1024,16]{1,0:T(8,128)}, u32[]{:S(2)}) copy-start(s32[1024,16]{1,0:T(8,128)} %get-tuple-element.10) | copy-start | bytes 196612
  311.6 3.9 copy-start.21
  312.0 5.3 %copy-start.63 = (f32[8]{0:T(128)S(1)}, f32[8]{0:T(128)}, u32[]{:S(2)}) copy-start(f32[8]{0:T(128)} %copy-done.62) | copy-start | bytes 100
  312.0 5.3 %copy-start.43 = (f32[8]{0:T(128)S(1)}, f32[8]{0:T(128)}, u32[]{:S(2)}) copy-start(f32[8]{0:T(128)} %copy-done.42) | copy-start | bytes 100
  312.0 5.3 %copy-start.51 = (f32[8]{0:T(128)S(1)}, f32[8]{0:T(128)}, u32[]{:S(2)}) copy-start(f32[8]{0:T(128)} %copy-done.50) | copy-start | bytes 100
  313.6 6.0 %copy-start.3 = (bf16[32,32,768]{2,1,0:T(8,128)(2,1)S(1)}, bf16[32,32,768]{2,1,0:T(8,128)(2,1)}, u32[]{:S(2)}) copy-start(bf16[32,32,768]{2,1,0:T(8,128)(2,1)} %param.13) | copy-start | bytes 4718596
  313.6 6.0 %copy-start.6 = (f32[8,32,768]{2,1,0:T(8,128)S(1)}, f32[8,32,768]{2,1,0:T(8,128)}, u32[]{:S(2)}) copy-start(f32[8,32,768]{2,1,0:T(8,128)} %reduce-scatter.4.cloned.1.call-done) | copy-start | bytes 2359300
  313.6 6.0 %copy-start.25 = (f32[768]{0:T(1024)S(1)}, f32[768]{0:T(1024)}, u32[]{:S(2)}) copy-start(f32[768]{0:T(1024)} %copy-done.24) | copy-start | bytes 9220
  313.6 6.0 %copy-start.27 = (f32[8,32]{1,0:T(8,128)S(1)}, f32[8,32]{1,0:T(8,128)}, u32[]{:S(2)}) copy-start(f32[8,32]{1,0:T(8,128)} %copy-done.26) | copy-start | bytes 3076
  314.7 5.3 %copy-start.34 = (f32[8,32]{1,0:T(8,128)S(1)}, f32[8,32]{1,0:T(8,128)}, u32[]{:S(2)}) copy-start(f32[8,32]{1,0:T(8,128)} %copy-done.33) | copy-start | bytes 3076
  314.7 5.3 %copy-start.32 = (f32[8,32]{1,0:T(8,128)S(1)}, f32[8,32]{1,0:T(8,128)}, u32[]{:S(2)}) copy-start(f32[8,32]{1,0:T(8,128)} %copy-done.31) | copy-start | bytes 3076
  320.0 2.9 copy-start.29
  321.1 51.9 %all-gather.8.cloned.1.call-start = ((), (), s32[]{:S(2)}) async-start(), calls=%async_computation.6 | async-start | bytes 1966080 | tf_op jit(solution)/shard_map/all_gather | solution.py:173
  321.3 4.1 copy-start.61
  321.3 4.1 copy-start.47
  321.3 4.1 copy-start.49
  322.6 5.1 %copy-start.5 = (bf16[16,64,768]{2,1,0:T(8,128)(2,1)S(1)}, bf16[16,64,768]{2,1,0:T(8,128)(2,1)}, u32[]{:S(2)}) copy-start(bf16[16,64,768]{2,1,0:T(8,128)(2,1)} %param.14) | copy-start | bytes 4718596
  322.6 5.1 %copy-start.7 = (f32[4,64,768]{2,1,0:T(8,128)S(1)}, f32[4,64,768]{2,1,0:T(8,128)}, u32[]{:S(2)}) copy-start(f32[4,64,768]{2,1,0:T(8,128)} %reduce-scatter.6.cloned.1.call-done) | copy-start | bytes 2359300
  322.6 5.2 %copy-start.23 = (f32[768]{0:T(1024)S(1)}, f32[768]{0:T(1024)}, u32[]{:S(2)}) copy-start(f32[768]{0:T(1024)} %copy-done.22) | copy-start | bytes 9220
  322.6 5.2 %copy-start.36 = (f32[4,64]{1,0:T(4,128)S(1)}, f32[4,64]{1,0:T(4,128)}, u32[]{:S(2)}) copy-start(f32[4,64]{1,0:T(4,128)} %copy-done.35) | copy-start | bytes 3076
  322.8 5.3 %copy-start.40 = (f32[4,64]{1,0:T(4,128)S(1)}, f32[4,64]{1,0:T(4,128)}, u32[]{:S(2)}) copy-start(f32[4,64]{1,0:T(4,128)} %copy-done.39) | copy-start | bytes 3076
  322.9 5.2 %copy-start.38 = (f32[4,64]{1,0:T(4,128)S(1)}, f32[4,64]{1,0:T(4,128)}, u32[]{:S(2)}) copy-start(f32[4,64]{1,0:T(4,128)} %copy-done.37) | copy-start | bytes 3076
  329.2 158.4 %reduce-scatter.8.cloned.1.call-start = ((), (), s32[]{:S(2)}) async-start(), calls=%async_computation.7 | async-start | bytes 9732096 | tf_op jit(solution)/shard_map/reduce_scatter | solution.py:202
  345.0 2.9 copy-start.13
  345.0 2.9 copy-start.58
  373.0 2.9 copy-start.59
  373.0 3.9 copy-start.66
  375.9 2.1 copy-start.64
  377.9 1.6 copy-start.69
  379.5 2.4 copy-start.17
  379.5 2.4 copy-start.68
  381.9 1.6 copy-start.70
  391.7 97.6 %copy-start.1 = (s32[32,15]{0,1:T(8,128)S(1)}, s32[32,15]{0,1:T(8,128)}, u32[]{:S(2)}) copy-start(s32[32,15]{0,1:T(8,128)} %param.24) | copy-start | bytes 5764
  (13 other events, 12.8 us)
Sparse Core Ops, SparseCore 0:
  18.8 40.7 reduce-scatter.3
  62.0 37.9 reduce-scatter.5
  105.2 65.5 all-gather.9
  321.2 23.8 all-gather.5
  346.6 26.3 all-gather.7
  391.8 95.7 reduce-scatter.7
where the time goes:
time: 497 us; the launch traced here: 496 us
  waiting for transfers between devices  264 us (53%)
  local copies, waits for them, and re-layouts  150 us (30%)
  matrix products  41.1 us (8%)
  other arithmetic  25.1 us (5%)
  between operations  15.2 us (3%)
    gather x3, local copies, waits for them, and re-layouts, body(): scores = jnp.take_along_axis(all_scores, cand_all, axis=1)  130 us
    reduce_scatter x1, waiting for transfers between devices, body(): lax.psum_scatter(weight_terms(), 'dp', scatter_dimension=0, tiled=True)  95.9 us
    all_gather x1, waiting for transfers between devices, body(): gathered = lax.all_gather(packed, ('dp', 'segment'), axis=0, tiled=False)  65.5 us
    reduce_scatter x1, waiting for transfers between devices, body(): lax.psum_scatter(passage_parts[5], 'segment', scatter_dimension=0, tiled=...  36.7 us
    reduce_scatter x1, waiting for transfers between devices, body(): lax.psum_scatter(query_parts[5], 'segment', scatter_dimension=0, tiled=True)  27.3 us
    all_gather x1, waiting for transfers between devices, body(): lax.all_gather(passage_share, 'segment', axis=0, tiled=True)  22.7 us
    all_gather x1, waiting for transfers between devices, body(): lax.all_gather(query_share, 'segment', axis=0, tiled=True)  15.6 us
    dot_general x6, matrix products, contract(): lax.dot_general(left, right, (((0,), (0,)), ((), ())), preferred_element_...  12.7 us
  transfers between devices with their start and end apart: 6, of which 6 were waited for; matrix products, arithmetic and copies ran while one was open for 5% of the time, Pallas kernels for 0%

commit v1 on v0

--- a/solution.py
+++ b/solution.py
@@ -8,6 +8,27 @@
 recall_depth = 5.0
 loss_scale = 16.0
 norm_eps = 1e-06
+
+
+def gather_around(x, axis, dim):
+    count, index, width = (lax.axis_size(axis), lax.axis_index(axis), x.shape[dim])
+    ahead = [(i, (i + 1) % count) for i in range(count)]
+    left = [(i, (i - 1) % count) for i in range(count)]
+    out = jnp.zeros((*x.shape[:dim], count * width, *x.shape[dim + 1 :]), x.dtype)
+    out = lax.dynamic_update_slice_in_dim(out, x, index * width, axis=dim)
+    from_left = from_right = x
+    middle = count // 2
+    for hop in range(1, middle + 1):
+        from_left = lax.ppermute(from_left, axis, ahead)
+        out = lax.dynamic_update_slice_in_dim(
+            out, from_left, (index - hop) % count * width, axis=dim
+        )
+        if hop < count - middle:
+            from_right = lax.ppermute(from_right, axis, left)
+            out = lax.dynamic_update_slice_in_dim(
+                out, from_right, (index + hop) % count * width, axis=dim
+            )
+    return out
 
 
 def inverse_rms(values):
@@ -169,7 +190,7 @@
     query_share = query_back(query_grad)[0].astype(jnp.bfloat16)
     passage_share = passage_back(passage_grad)[0].astype(jnp.bfloat16)
     query_rows, passage_rows = (
-        lax.all_gather(query_share, "segment", axis=0, tiled=True),
+        gather_around(query_share, "segment", 0),
         lax.all_gather(passage_share, "segment", axis=0, tiled=True),
     )
 

time: 497 us -> 478 us (0.962)
  waiting for transfers between devices: 264 us -> 236 us
  local copies, waits for them, and re-layouts: 150 us -> 159 us
    all_gather x1, waiting for transfers between devices: 22.7 us -> 0.01 us  [body(): lax.all_gather(passage_share, 'segment', axis=0, tiled=True)]
    ppermute x0 -> x3, waiting for transfers between devices: none -> 17.6 us  [the longest x2 17.6 us: gather_around(): from_left = lax.ppermute(from_left, axis, ahead)]
    all_gather x1 -> x0, waiting for transfers between devices: 15.6 us -> none  [body(): lax.all_gather(query_share, 'segment', axis=0, tiled=True)]
    reduce_scatter x1, waiting for transfers between devices: 95.9 us -> 89.7 us  [body(): lax.psum_scatter(weight_terms(), 'dp', scatter_dimension=0, tiled=True)]
    unnamed x143 -> x155, local copies, waits for them, and re-layouts: 9.62 us -> 12.1 us
  transfers between devices with their start and end apart: 6 -> 8, of which waited for: 6 -> 6; matrix products, arithmetic and copies ran while one was open for 5% -> 7% of each run, Pallas kernels for 0% -> 0%
where the time goes in v1:
time: 478 us
  waiting for transfers between devices  236 us (49%)
  local copies, waits for them, and re-layouts  159 us (33%)
  matrix products  40.6 us (8%)
  other arithmetic  23.1 us (5%)
  between operations  14.9 us (3%)
    gather x3, local copies, waits for them, and re-layouts, body(): scores = jnp.take_along_axis(all_scores, cand_all, axis=1)  130 us
    reduce_scatter x1, waiting for transfers between devices, body(): lax.psum_scatter(weight_terms(), 'dp', scatter_dimension=0, tiled=True)  89.7 us
    all_gather x1, waiting for transfers between devices, body(): gathered = lax.all_gather(packed, ('dp', 'segment'), axis=0, tiled=False)  65 us
    reduce_scatter x1, waiting for transfers between devices, body(): lax.psum_scatter(passage_parts[5], 'segment', scatter_dimension=0, tiled=...  36.7 us
    reduce_scatter x1, waiting for transfers between devices, body(): lax.psum_scatter(query_parts[5], 'segment', scatter_dimension=0, tiled=True)  27.3 us
    ppermute x2, waiting for transfers between devices, gather_around(): from_left = lax.ppermute(from_left, axis, ahead)  17.6 us
    dot_general x6, matrix products, contract(): lax.dot_general(left, right, (((0,), (0,)), ((), ())), preferred_element_...  14.5 us
    unnamed x155, local copies, waits for them, and re-layouts  12.1 us
  transfers between devices with their start and end apart: 8, of which 6 were waited for; matrix products, arithmetic and copies ran while one was open for 7% of the time, Pallas kernels for 0%

profile of v1, /device:TPU:0, one launch (start us, length us, event | category | flops | bytes accessed | tf_op | source)
XLA Modules:
  0.0 477.6 jit_solution(2228618564687936686)
XLA Ops:
  7.2 0.8 slice_reduce_fusion.5
  8.1 1.9 fusion
  10.5 1.0 fusion.56
  11.6 0.8 copy-done.64
  12.5 2.6 multiply_convert_fusion.3
  15.1 1.0 copy-done.22
  16.1 2.6 fusion.50
  18.8 1.3 copy-done.4
  20.9 0.6 copy-done.63
  21.5 1.0 fusion.48
  22.9 2.7 multiply_convert_fusion.2
  25.6 1.0 copy-done.23
  26.6 2.7 fusion.42
  29.3 0.6 copy-done.51
  30.6 0.8 fusion.121
  31.4 0.8 fusion.119
  32.3 27.3 %reduce-scatter.4.cloned.1.call-done = f32[8,32,768]{2,1,0:T(8,128)} async-done(((f32[32,32,768]{2,1,0:T(8,128)}), f32[8,32,768]{2,1,0:T(8,128)}) %reduce-scatter.4.cloned.1.call-update) | async-done | bytes 786448 | tf_op jit(solution)/shard_map/reduce_scatter | solution.py:121
  59.6 1.5 multiply_reduce_fusion.5
  61.1 1.4 multiply_reduce_fusion.4
  62.6 0.7 multiply_reduce_fusion.7
  63.4 36.7 %reduce-scatter.6.cloned.1.call-done = f32[4,64,768]{2,1,0:T(8,128)} async-done(((f32[16,64,768]{2,1,0:T(8,128)}), f32[4,64,768]{2,1,0:T(8,128)}) %reduce-scatter.6.cloned.1.call-update) | async-done | bytes 786448 | tf_op jit(solution)/shard_map/reduce_scatter | solution.py:122
  100.0 1.5 multiply_reduce_fusion.3
  101.6 1.4 multiply_reduce_fusion.2
  103.0 0.7 multiply_reduce_fusion.9
  104.4 0.6 maximum_bitcast_fusion.3
  105.8 65.0 %all-gather.7.cloned.1.call-done = bf16[128,13,768]{2,1,0:T(8,128)(2,1)} async-done(((bf16[1,13,768]{2,1,0:T(8,128)(2,1)}), bf16[128,13,768]{2,1,0:T(8,128)(2,1)}) %all-gather.7.cloned.1.call-update) | async-done | bytes 2555920 | tf_op jit(solution)/shard_map/all_gather | solution.py:149
  170.8 1.8 slice.100
  173.2 0.9 slice_reduce_fusion.1
  174.4 1.8 slice.106
  176.2 1.3 slice.105
  177.7 0.8 copy.43
  178.6 0.6 constant_dynamic-slice_fusion
  179.3 0.9 copy-done.10
  180.2 2.4 fusion.123
  182.7 129.5 %gather_fusion = f32[16384]{0:T(1024)S(1)} fusion(f32[1024,512]{1,0:T(8,128)S(1)} %fusion.123, s32[16384]{0:T(1024)S(1)} %reshape.165), kind=kCustom, calls=%fused_computation | custom fusion | bytes 262144 | tf_op jit(solution)/shard_map/jit(take_along_axis)/gather | solution.py:165
  312.8 0.6 select_reduce_fusion
  313.5 1.0 fusion.117
  315.8 0.6 copy-done.61
  316.4 1.0 fusion.28
  317.9 1.3 broadcast_in_dim.77
  319.2 1.1 constant_dynamic-update-slice_fusion.3
  320.6 3.0 collective-permute-start.1
  323.9 2.2 multiply_reduce_fusion.8
  326.2 2.3 fusion.31
  328.9 1.0 fusion.41
  330.0 2.9 collective-permute-done
  332.9 1.8 constant_dynamic-update-slice_fusion.2
  334.7 1.8 constant_dynamic-update-slice_fusion.1
  336.5 14.7 %collective-permute-done.2 = bf16[8,32,768]{2,1,0:T(8,128)(2,1)S(1)} collective-permute-done((bf16[8,32,768]{2,1,0:T(8,128)(2,1)}, bf16[8,32,768]{2,1,0:T(8,128)(2,1)S(1)}, u32[]{:S(2)}, u32[]{:S(2)}) %collective-permute-start.2) | collective-permute-done | bytes 393248 | tf_op jit(solution)/shard_map/ppermute | solution.py:22
  351.2 0.8 constant_dynamic-update-slice_fusion
  352.0 2.8 convolution_bitcast_fusion.1
  354.9 2.6 fusion.52
  357.5 2.3 convolution_bitcast_fusion.3
  359.8 3.1 convolution_bitcast_fusion.5
  362.9 2.8 convolution_bitcast_fusion
  365.7 1.0 fusion.44
  367.1 0.7 copy-done.74
  367.8 1.1 convolution_bitcast_fusion.2
  369.4 2.4 convolution_bitcast_fusion.4
  372.1 1.1 copy-done.21
  373.5 1.1 copy-done.20
  374.9 4.8 pad_maximum_fusion
  379.7 89.7 %reduce-scatter.8.cloned.1.call-done = f32[24,3,2,512]{3,0,2,1:T(8,128)} async-done(((f32[768,3,2,512]{3,0,2,1:T(8,128)}), f32[24,3,2,512]{3,0,2,1:T(8,128)}) %reduce-scatter.8.cloned.1.call-update) | async-done | bytes 294928 | tf_op jit(solution)/shard_map/reduce_scatter | solution.py:223
  469.3 1.7 slice_bitcast_fusion
  (208 shorter events, 10.4 us)
Async XLA Ops:
  7.2 23.0 %copy-start = (s32[32,15]{0,1:T(8,128)S(1)}, s32[32,15]{0,1:T(8,128)}, u32[]{:S(2)}) copy-start(s32[32,15]{0,1:T(8,128)} %param.24) | copy-start | bytes 5764
  7.2 2.8 copy-start.2
  7.2 52.4 %reduce-scatter.4.cloned.1.call-start = ((), (), s32[]{:S(2)}) async-start(), calls=%async_computation.3 | async-start | bytes 3932160 | tf_op jit(solution)/shard_map/reduce_scatter | solution.py:121
  8.1 2.4 copy-start.62
  10.5 2.0 copy-start.64
  12.4 2.6 copy-start.71
  12.5 3.6 copy-start.13
  18.7 81.3 %reduce-scatter.6.cloned.1.call-start = ((), (), s32[]{:S(2)}) async-start(), calls=%async_computation.4 | async-start | bytes 3932160 | tf_op jit(solution)/shard_map/reduce_scatter | solution.py:122
  22.9 2.7 copy-start.73
  22.9 3.7 copy-start.14
  29.2 3.0 copy-start.47
  29.3 141.5 %all-gather.7.cloned.1.call-start = ((), (), s32[]{:S(2)}) async-start(), calls=%async_computation.7 | async-start | bytes 3170304 | tf_op jit(solution)/shard_map/all_gather | solution.py:149
  31.4 70.1 %copy-start.40 = (f32[4,64]{1,0:T(4,128)}, f32[4,64]{1,0:T(4,128)S(1)}, u32[]{:S(2)}) copy-start(f32[4,64]{1,0:T(4,128)S(1)} %get-tuple-element.16) | copy-start | bytes 3076
  31.4 71.6 %copy-start.53 = (f32[4]{0:T(128)}, f32[4]{0:T(128)S(1)}, u32[]{:S(2)}) copy-start(f32[4]{0:T(128)S(1)} %get-tuple-element.15) | copy-start | bytes 52
  32.2 69.3 %copy-start.31 = (f32[8,32]{1,0:T(8,128)}, f32[8,32]{1,0:T(8,128)S(1)}, u32[]{:S(2)}) copy-start(f32[8,32]{1,0:T(8,128)S(1)} %get-tuple-element.14) | copy-start | bytes 3076
  32.2 69.3 %copy-start.57 = (f32[8]{0:T(128)}, f32[8]{0:T(128)S(1)}, u32[]{:S(2)}) copy-start(f32[8]{0:T(128)S(1)} %get-tuple-element.13) | copy-start | bytes 100
  32.3 69.2 %copy-start.29 = (f32[768]{0:T(1024)}, f32[768]{0:T(1024)S(1)}, u32[]{:S(2)}) copy-start(f32[768]{0:T(1024)S(1)} %get-tuple-element.5) | copy-start | bytes 9220
  32.3 69.3 %copy-start.27 = (f32[768]{0:T(1024)}, f32[768]{0:T(1024)S(1)}, u32[]{:S(2)}) copy-start(f32[768]{0:T(1024)S(1)} %get-tuple-element.6) | copy-start | bytes 9220
  59.6 3.0 copy-start.59
  63.3 109.3 %copy-start.25 = (f32[8,768]{1,0:T(8,128)}, f32[8,768]{1,0:T(8,128)S(1)}, u32[]{:S(2)}) copy-start(f32[8,768]{1,0:T(8,128)S(1)} %get-tuple-element.29) | copy-start | bytes 73732
  63.3 109.3 %copy-start.69 = (f32[8]{0:T(128)}, f32[8]{0:T(128)S(1)}, u32[]{:S(2)}) copy-start(f32[8]{0:T(128)S(1)} %get-tuple-element.28) | copy-start | bytes 100
  63.3 109.3 %copy-start.48 = (f32[8]{0:T(128)}, f32[8]{0:T(128)S(1)}, u32[]{:S(2)}) copy-start(f32[8]{0:T(128)S(1)} %add_rsqrt_fusion.3) | copy-start | bytes 100
  100.0 3.0 copy-start.60
  101.5 71.2 %copy-start.44 = (f32[4,64]{1,0:T(4,128)}, f32[4,64]{1,0:T(4,128)S(1)}, u32[]{:S(2)}) copy-start(f32[4,64]{1,0:T(4,128)S(1)} %multiply_reduce_fusion.3) | copy-start | bytes 3076
  101.5 71.2 %copy-start.42 = (f32[4,64]{1,0:T(4,128)}, f32[4,64]{1,0:T(4,128)S(1)}, u32[]{:S(2)}) copy-start(f32[4,64]{1,0:T(4,128)S(1)} %fusion.95) | copy-start | bytes 3076
  103.8 69.0 %copy-start.55 = (f32[4]{0:T(128)}, f32[4]{0:T(128)S(1)}, u32[]{:S(2)}) copy-start(f32[4]{0:T(128)S(1)} %add_rsqrt_fusion.2) | copy-start | bytes 52
  105.1 257.8 %all-gather.5.cloned.1.call-start = ((), (), s32[]{:S(2)}) async-start(), calls=%async_computation.5 | async-start | bytes 1966080 | tf_op jit(solution)/shard_map/all_gather | solution.py:194
  173.1 3.1 copy-start.12
  174.4 4.2 copy-start.8
  182.6 129.7 %copy-start.9 = (s32[1024,16]{1,0:T(8,128)S(1)}, s32[1024,16]{1,0:T(8,128)}, u32[]{:S(2)}) copy-start(s32[1024,16]{1,0:T(8,128)} %copy-done.8) | copy-start | bytes 196612
  313.5 1.6 copy-start.46
  313.5 1.7 copy-start.11
  313.5 1.7 copy-start.26
  314.7 1.7 copy-start.61
  314.8 2.6 copy-start.3
  314.8 2.6 copy-start.6
  314.8 2.6 copy-start.30
  314.8 2.7 copy-start.32
  314.8 3.0 copy-start.39
  315.8 3.4 copy-start.37
  317.8 5.9 %copy-start.24 = (s32[1024,16]{0,1:T(8,128)S(1)}, s32[1024,16]{0,1:T(8,128)}, u32[]{:S(2)}) copy-start(s32[1024,16]{0,1:T(8,128)} %copy.43) | copy-start | bytes 196612
  317.8 5.9 %copy-start.50 = (s32[4]{0:T(128)S(1)}, s32[4]{0:T(128)}, u32[]{:S(2)}) copy-start(s32[4]{0:T(128)} %iota_add_fusion) | copy-start | bytes 52
  317.8 6.0 %copy-start.34 = (f32[4,768]{1,0:T(4,128)S(1)}, f32[4,768]{1,0:T(4,128)}, u32[]{:S(2)}) copy-start(f32[4,768]{1,0:T(4,128)} %copy-done.33) | copy-start | bytes 36868
  319.2 7.0 %copy-start.68 = (f32[4]{0:T(128)S(1)}, f32[4]{0:T(128)}, u32[]{:S(2)}) copy-start(f32[4]{0:T(128)} %copy-done.67) | copy-start | bytes 52
  319.2 7.0 %copy-start.54 = (f32[4]{0:T(128)S(1)}, f32[4]{0:T(128)}, u32[]{:S(2)}) copy-start(f32[4]{0:T(128)} %copy-done.53) | copy-start | bytes 52
  319.2 7.0 %copy-start.56 = (f32[4]{0:T(128)S(1)}, f32[4]{0:T(128)}, u32[]{:S(2)}) copy-start(f32[4]{0:T(128)} %copy-done.55) | copy-start | bytes 52
  320.3 8.2 %copy-start.5 = (bf16[16,64,768]{2,1,0:T(8,128)(2,1)S(1)}, bf16[16,64,768]{2,1,0:T(8,128)(2,1)}, u32[]{:S(2)}) copy-start(bf16[16,64,768]{2,1,0:T(8,128)(2,1)} %param.14) | copy-start | bytes 4718596
  320.3 8.3 %copy-start.7 = (f32[4,64,768]{2,1,0:T(8,128)S(1)}, f32[4,64,768]{2,1,0:T(8,128)}, u32[]{:S(2)}) copy-start(f32[4,64,768]{2,1,0:T(8,128)} %reduce-scatter.6.cloned.1.call-done) | copy-start | bytes 2359300
  320.3 8.3 %copy-start.28 = (f32[768]{0:T(1024)S(1)}, f32[768]{0:T(1024)}, u32[]{:S(2)}) copy-start(f32[768]{0:T(1024)} %copy-done.27) | copy-start | bytes 9220
  320.3 8.3 %copy-start.41 = (f32[4,64]{1,0:T(4,128)S(1)}, f32[4,64]{1,0:T(4,128)}, u32[]{:S(2)}) copy-start(f32[4,64]{1,0:T(4,128)} %copy-done.40) | copy-start | bytes 3076
  320.3 12.6 %collective-permute-start = (bf16[8,32,768]{2,1,0:T(8,128)(2,1)S(1)}, bf16[8,32,768]{2,1,0:T(8,128)(2,1)}, u32[]{:S(2)}, u32[]{:S(2)}) collective-permute-start(bf16[8,32,768]{2,1,0:T(8,128)(2,1)S(1)} %get-tuple-element.8), channel_id=1, source_target_pairs={{0,32},{32,64},{64,96},{96,0},{1,33},{33,65},{65,97},{97,1},{2,34}... | collective-permute-start | bytes 1179656 | tf_op jit(solution)/shard_map/ppermute | solution.py:22
  320.6 14.1 %collective-permute-start.1 = (bf16[8,32,768]{2,1,0:T(8,128)(2,1)S(1)}, bf16[8,32,768]{2,1,0:T(8,128)(2,1)}, u32[]{:S(2)}, u32[]{:S(2)}) collective-permute-start(bf16[8,32,768]{2,1,0:T(8,128)(2,1)S(1)} %get-tuple-element.8), channel_id=1, source_target_pairs={{0,96},{32,0},{64,32},{96,64},{1,97},{33,1},{65,33},{97,65},{2,98}... | collective-permute-start | bytes 1179656 | tf_op jit(solution)/shard_map/ppermute | solution.py:27
  323.7 5.1 %copy-start.45 = (f32[4,64]{1,0:T(4,128)S(1)}, f32[4,64]{1,0:T(4,128)}, u32[]{:S(2)}) copy-start(f32[4,64]{1,0:T(4,128)} %copy-done.44) | copy-start | bytes 3076
  323.9 5.0 %copy-start.43 = (f32[4,64]{1,0:T(4,128)S(1)}, f32[4,64]{1,0:T(4,128)}, u32[]{:S(2)}) copy-start(f32[4,64]{1,0:T(4,128)} %copy-done.42) | copy-start | bytes 3076
  330.0 139.4 %reduce-scatter.8.cloned.1.call-start = ((), (), s32[]{:S(2)}) async-start(), calls=%async_computation.6 | async-start | bytes 9732096 | tf_op jit(solution)/shard_map/reduce_scatter | solution.py:223
  332.9 18.3 %collective-permute-start.2 = (bf16[8,32,768]{2,1,0:T(8,128)(2,1)}, bf16[8,32,768]{2,1,0:T(8,128)(2,1)S(1)}, u32[]{:S(2)}, u32[]{:S(2)}) collective-permute-start(bf16[8,32,768]{2,1,0:T(8,128)(2,1)} %collective-permute-done), channel_id=1, source_target_pairs={{0,32},{32,64},{64,96},{96,0},{1,33},{33,65},{65,97},{97,1},{2,34}... | collective-permute-start | bytes 1179656 | tf_op jit(solution)/shard_map/ppermute | solution.py:22
  352.0 2.9 copy-start.15
  354.9 2.6 copy-start.17
  354.9 2.6 copy-start.72
  357.5 2.3 copy-start.75
  362.9 2.8 copy-start.66
  365.7 2.1 copy-start.74
  367.8 1.6 copy-start.76
  379.7 91.4 %copy-start.1 = (s32[32,15]{0,1:T(8,128)S(1)}, s32[32,15]{0,1:T(8,128)}, u32[]{:S(2)}) copy-start(s32[32,15]{0,1:T(8,128)} %param.24) | copy-start | bytes 5764
  (21 other events, 24.0 us)
Sparse Core Ops, SparseCore 0:
  18.8 40.7 reduce-scatter.3
  62.0 37.9 reduce-scatter.5
  105.2 65.5 all-gather.6
  330.1 27.5 all-gather.4
  379.8 89.5 reduce-scatter.7
